TPU v7x, 512 devices: a whole 4x4x16 slice. The times are simulated.
512 devices in a mesh: dp: 16 (over z_lo, core), ctx: 32 (over y, x, z_hi).
Axes of the slice: x: 4, y: 4, z: 16 (z_hi: 2, z_lo: 8; z = z_hi * 8 + z_lo), core: 2. Of those that a mesh axis runs over, the one named last changes fastest.
Arguments:
- queries: bfloat16 [131072, 256], P(('dp', 'ctx')), parts along dimension 0, may hold values from -6 to 6
- keys: bfloat16 [131072, 256], P(('dp', 'ctx')), parts along dimension 0, may hold values from -6 to 6
- values: bfloat16 [131072, 256], P(('dp', 'ctx')), parts along dimension 0, may hold values from -6 to 6
- out_grad: bfloat16 [131072, 256], P(('dp', 'ctx')), parts along dimension 0, may hold values from -16 to 16
- block_list: int32 [1024, 7], P(('dp', 'ctx')), parts along dimension 0, may hold values from -1 to 63, as said below
- causal: int32 [1024], P(('dp', 'ctx')), parts along dimension 0, may hold values 0 or 1
Outputs:
- query_grad: bfloat16 [131072, 256], P(('dp', 'ctx')), parts along dimension 0
- key_grad: bfloat16 [131072, 256], P(('dp', 'ctx')), parts along dimension 0
- value_grad: bfloat16 [131072, 256], P(('dp', 'ctx')), parts along dimension 0
There are 16 independent parts, one for each index of `dp`. A program takes and returns all parts, laid end to end along the dimension named above; each array names one. Nothing has to cross between parts.
Inputs may be any that keep to these rules, and one draw needn't show every extreme that they name: `block_list`: entry 0 of block b is b; entry j, for j from 1 to 6, is b - 2**(j-1) or -1, and is -1 where that would be negative.
All inputs are finite; a program needn't handle non-finite values. No bound on the sum of `causal` on one device may be relied on, other than what follows from the above.
Results may differ from a plain program's by a relative error of at most 0.034.
Values may be sent and summed in bfloat16 or wider, within the bound.
No kernel may reach another device: no remote copies, remote signals or barrier semaphores. Data moves between devices by JAX's collectives and lax.ppermute only.
A program may use at most 64 MiB of HBM per device.

v0:
```python
import jax
import jax.numpy as jnp
from jax import lax
from jax.sharding import PartitionSpec as P

BLOCK = 128
HEADS = 2


def from_behind(value, axis, steps):
    count = lax.axis_size(axis)
    initial, last = (max(0, -steps), min(count, count - steps))
    return lax.ppermute(value, axis, [(source, source + steps) for source in range(initial, last)])


def return_terms(key_terms, value_terms, hop_count):
    return from_behind((key_terms, value_terms), "ctx", -hop_count)


def window_of(earlier, own_shard, reach, blocks_here):
    joined = jnp.concatenate([earlier, own_shard], 0)
    start = (blocks_here - reach) * BLOCK
    return joined[start : start + own_shard.shape[0]]


def on_device(queries, keys, values, out_grad, block_list, causal):
    tok_rows, feat = queries.shape
    blocks_here = tok_rows // BLOCK
    entries = block_list.shape[1]
    head_size = feat // HEADS
    scale = head_size ** (-0.5)

    def to_blocks(array):
        return array.reshape(blocks_here, BLOCK, HEADS, head_size)

    q_blocks = to_blocks(queries)
    g_blocks = to_blocks(out_grad)
    positions = jnp.arange(BLOCK)
    lower = positions[:, None] >= positions[None, :]
    self_mask = jnp.where(causal[:, None, None] > 0, lower[None], True)
    self_mask = self_mask & (block_list[:, 0] >= 0)[:, None, None]
    score_list = []
    dprob_list = []
    kept_keys = []
    near_pair = from_behind((keys, values), "ctx", 1)
    last_pair = near_pair
    for level in range(entries):
        if level == 0:
            level_keys, level_values = (keys, values)
            mask = self_mask[:, None, :, :]
        else:
            reach = 2 ** (level - 1)
            if reach <= blocks_here:
                level_keys = window_of(near_pair[0], keys, reach, blocks_here)
                level_values = window_of(near_pair[1], values, reach, blocks_here)
            else:
                distance = reach // blocks_here
                last_pair = from_behind((keys, values), "ctx", distance)
                level_keys, level_values = last_pair
            mask = (block_list[:, level] >= 0)[:, None, None, None]
        kept_keys.append(level_keys)
        scores = (
            jnp.einsum(
                "bthd,buhd->bhtu",
                q_blocks,
                to_blocks(level_keys),
                preferred_element_type=jnp.float32,
            )
            * scale
        )
        score_list.append(jnp.where(mask, scores, -jnp.inf))
        dprob_list.append(
            jnp.einsum(
                "bthd,buhd->bhtu",
                g_blocks,
                to_blocks(level_values),
                preferred_element_type=jnp.float32,
            )
        )
    top = score_list[0].max(axis=3)
    for level in range(1, entries):
        top = jnp.maximum(top, score_list[level].max(axis=3))
    total = jnp.zeros_like(top)
    for level in range(entries):
        total = total + jnp.sum(jnp.exp(score_list[level] - top[..., None]), axis=3)
    lse = top + jnp.log(total)
    delta = jnp.zeros_like(top)
    for level in range(entries):
        weights = jnp.exp(score_list[level] - lse[..., None]).astype(jnp.bfloat16)
        delta = delta + jnp.sum(weights.astype(jnp.float32) * dprob_list[level], axis=3)
    query_sum = jnp.zeros((blocks_here, BLOCK, HEADS, head_size), jnp.float32)
    key_local = jnp.zeros((tok_rows, feat), jnp.float32)
    value_local = jnp.zeros((tok_rows, feat), jnp.float32)
    key_near = jnp.zeros((tok_rows, feat), jnp.float32)
    value_near = jnp.zeros((tok_rows, feat), jnp.float32)
    for level in range(entries):
        reach = 2 ** (level - 1) if level > 0 else 0
        level_keys = kept_keys[level]
        probs = jnp.exp(score_list[level] - lse[..., None])
        weights = probs.astype(jnp.bfloat16)
        dscores = (probs * (dprob_list[level] - delta[..., None])).astype(jnp.bfloat16)
        query_sum = query_sum + jnp.einsum(
            "bhtu,buhd->bthd", dscores, to_blocks(level_keys), preferred_element_type=jnp.float32
        )
        key_terms = (
            jnp.einsum("bhtu,bthd->buhd", dscores, q_blocks, preferred_element_type=jnp.float32)
            * scale
        ).reshape(tok_rows, feat)
        value_terms = jnp.einsum(
            "bhtu,bthd->buhd", weights, g_blocks, preferred_element_type=jnp.float32
        ).reshape(tok_rows, feat)
        if level == 0:
            key_local = key_terms
            value_local = value_terms
        elif reach < blocks_here:
            cut = reach * BLOCK
            pad_own = jnp.zeros((cut, feat), jnp.float32)
            pad_near = jnp.zeros((tok_rows - cut, feat), jnp.float32)
            key_local = key_local + jnp.concatenate([key_terms[cut:], pad_own], 0)
            value_local = value_local + jnp.concatenate([value_terms[cut:], pad_own], 0)
            key_near = jnp.concatenate([pad_near, key_terms[:cut]], 0)
            value_near = jnp.concatenate([pad_near, value_terms[:cut]], 0)
        elif reach == blocks_here:
            key_near = key_near + key_terms
            value_near = value_near + value_terms
        else:
            back_keys, back_values = return_terms(
                key_terms.astype(jnp.bfloat16),
                value_terms.astype(jnp.bfloat16),
                reach // blocks_here,
            )
            key_local = key_local + back_keys.astype(jnp.float32)
            value_local = value_local + back_values.astype(jnp.float32)
    back_keys, back_values = return_terms(
        key_near.astype(jnp.bfloat16), value_near.astype(jnp.bfloat16), 1
    )
    key_grad = (key_local + back_keys.astype(jnp.float32)).astype(jnp.bfloat16)
    value_grad = (value_local + back_values.astype(jnp.float32)).astype(jnp.bfloat16)
    query_grad = (query_sum * scale).astype(jnp.bfloat16).reshape(tok_rows, feat)
    return (query_grad, key_grad, value_grad)


def solution(mesh):
    return jax.shard_map(
        on_device,
        mesh=mesh,
        in_specs=(
            P(("dp", "ctx"), None),
            P(("dp", "ctx"), None),
            P(("dp", "ctx"), None),
            P(("dp", "ctx"), None),
            P(("dp", "ctx"), None),
            P(("dp", "ctx")),
        ),
        out_specs=(P(("dp", "ctx"), None), P(("dp", "ctx"), None), P(("dp", "ctx"), None)),
        check_vma=False,
    )
```

profile of v0, /device:TPU:46, one launch (start us, length us, event | category | flops | bytes accessed | tf_op | source)
XLA Modules:
  0.0 140.6 jit_solution(15301418070204012788)
XLA Ops:
  0.6 14.8 %collective-permute-start = (bf16[256,256]{1,0:T(8,128)(2,1)}, bf16[256,256]{1,0:T(8,128)(2,1)S(1)}, u32[]{:S(2)}, u32[]{:S(2)}) collective-permute-start(bf16[256,256]{1,0:T(8,128)(2,1)} %param.7), channel_id=1, source_target_pairs={{0,1},{1,2},{2,3},{3,4},{4,5},{5,6},{6,7},{7,8},{8,9},{9,10},{10,1... | collective-permute-start | bytes 393224 | tf_op jit(solution)/shard_map/ppermute | solution.py:13
  15.5 4.2 %collective-permute-start.4 = (bf16[256,256]{1,0:T(8,128)(2,1)}, bf16[256,256]{1,0:T(8,128)(2,1)S(1)}, u32[]{:S(2)}, u32[]{:S(2)}) collective-permute-start(bf16[256,256]{1,0:T(8,128)(2,1)} %param.7), channel_id=1, source_target_pairs={{0,16},{1,17},{2,18},{3,19},{4,20},{5,21},{6,22},{7,23},{8,24},{9,... | collective-permute-start | bytes 393224 | tf_op jit(solution)/shard_map/ppermute | solution.py:13
  19.7 1.9 %collective-permute-start.3 = (bf16[256,256]{1,0:T(8,128)(2,1)}, bf16[256,256]{1,0:T(8,128)(2,1)S(1)}, u32[]{:S(2)}, u32[]{:S(2)}) collective-permute-start(bf16[256,256]{1,0:T(8,128)(2,1)} %param.7), channel_id=1, source_target_pairs={{0,8},{1,9},{2,10},{3,11},{4,12},{5,13},{6,14},{7,15},{8,16},{9,17... | collective-permute-start | bytes 393224 | tf_op jit(solution)/shard_map/ppermute | solution.py:13
  21.6 2.7 %collective-permute-start.2 = (bf16[256,256]{1,0:T(8,128)(2,1)}, bf16[256,256]{1,0:T(8,128)(2,1)S(1)}, u32[]{:S(2)}, u32[]{:S(2)}) collective-permute-start(bf16[256,256]{1,0:T(8,128)(2,1)} %param.7), channel_id=1, source_target_pairs={{0,4},{1,5},{2,6},{3,7},{4,8},{5,9},{6,10},{7,11},{8,12},{9,13},{1... | collective-permute-start | bytes 393224 | tf_op jit(solution)/shard_map/ppermute | solution.py:13
  24.3 4.0 %collective-permute-start.1 = (bf16[256,256]{1,0:T(8,128)(2,1)}, bf16[256,256]{1,0:T(8,128)(2,1)S(1)}, u32[]{:S(2)}, u32[]{:S(2)}) collective-permute-start(bf16[256,256]{1,0:T(8,128)(2,1)} %param.7), channel_id=1, source_target_pairs={{0,2},{1,3},{2,4},{3,5},{4,6},{5,7},{6,8},{7,9},{8,10},{9,11},{10,... | collective-permute-start | bytes 393224 | tf_op jit(solution)/shard_map/ppermute | solution.py:13
  32.7 7.3 %collective-permute-start.5 = (bf16[256,256]{1,0:T(8,128)(2,1)S(1)}, bf16[256,256]{1,0:T(8,128)(2,1)S(1)}, u32[]{:S(2)}, u32[]{:S(2)}) collective-permute-start(bf16[256,256]{1,0:T(8,128)(2,1)S(1)} %copy-done.6), channel_id=1, source_target_pairs={{0,1},{1,2},{2,3},{3,4},{4,5},{5,6},{6,7},{7,8},{8,9},{9,10},{10,1... | collective-permute-start | bytes 393224 | tf_op jit(solution)/shard_map/ppermute | solution.py:13
  41.2 4.2 %collective-permute-start.9 = (bf16[256,256]{1,0:T(8,128)(2,1)S(1)}, bf16[256,256]{1,0:T(8,128)(2,1)S(1)}, u32[]{:S(2)}, u32[]{:S(2)}) collective-permute-start(bf16[256,256]{1,0:T(8,128)(2,1)S(1)} %copy-done.6), channel_id=1, source_target_pairs={{0,16},{1,17},{2,18},{3,19},{4,20},{5,21},{6,22},{7,23},{8,24},{9,... | collective-permute-start | bytes 393224 | tf_op jit(solution)/shard_map/ppermute | solution.py:13
  46.0 1.9 %collective-permute-start.8 = (bf16[256,256]{1,0:T(8,128)(2,1)S(1)}, bf16[256,256]{1,0:T(8,128)(2,1)S(1)}, u32[]{:S(2)}, u32[]{:S(2)}) collective-permute-start(bf16[256,256]{1,0:T(8,128)(2,1)S(1)} %copy-done.6), channel_id=1, source_target_pairs={{0,8},{1,9},{2,10},{3,11},{4,12},{5,13},{6,14},{7,15},{8,16},{9,17... | collective-permute-start | bytes 393224 | tf_op jit(solution)/shard_map/ppermute | solution.py:13
  48.6 2.7 %collective-permute-start.7 = (bf16[256,256]{1,0:T(8,128)(2,1)S(1)}, bf16[256,256]{1,0:T(8,128)(2,1)S(1)}, u32[]{:S(2)}, u32[]{:S(2)}) collective-permute-start(bf16[256,256]{1,0:T(8,128)(2,1)S(1)} %copy-done.6), channel_id=1, source_target_pairs={{0,4},{1,5},{2,6},{3,7},{4,8},{5,9},{6,10},{7,11},{8,12},{9,13},{1... | collective-permute-start | bytes 393224 | tf_op jit(solution)/shard_map/ppermute | solution.py:13
  52.1 3.8 %collective-permute-start.6 = (bf16[256,256]{1,0:T(8,128)(2,1)S(1)}, bf16[256,256]{1,0:T(8,128)(2,1)}, u32[]{:S(2)}, u32[]{:S(2)}) collective-permute-start(bf16[256,256]{1,0:T(8,128)(2,1)S(1)} %copy-done.6), channel_id=1, source_target_pairs={{0,2},{1,3},{2,4},{3,5},{4,6},{5,7},{6,8},{7,9},{8,10},{9,11},{10,... | collective-permute-start | bytes 393224 | tf_op jit(solution)/shard_map/ppermute | solution.py:13
  64.8 1.6 %reshape.251 = bf16[2,128,2,128]{3,2,1,0:T(2,128)(2,1)} reshape(bf16[256,256]{1,0:T(8,128)(2,1)} %collective-permute-done.6) | data formatting | bytes 262144 | tf_op jit(solution)/shard_map/reshape | solution.py:34
  68.2 1.6 %reshape.249 = bf16[2,128,2,128]{3,2,1,0:T(2,128)(2,1)} reshape(bf16[256,256]{1,0:T(8,128)(2,1)} %pad_maximum_fusion) | data formatting | bytes 262144 | tf_op jit(solution)/shard_map/reshape | solution.py:34
  69.8 1.8 %multiply_reduce_fusion.5 = (f32[2,2,128]{2,1,0:T(2,128)S(1)}, f32[2,2,128,128]{3,2,1,0:T(8,128)}) fusion(f32[2,2,128,128]{3,2,1,0:T(8,128)S(1)} %get-tuple-element.45, f32[2,2,128]{2,1,0:T(2,128)S(1)} %log_add_fusion, bf16[2,128,2,128]{3,2,1,0:T(2,128)(2,1)S(1)} %reshape.247, bf16[2,128,2,128]{3,2,1,0:T(2,128)(2,1)} %reshape.249), kind=kOutput, calls=%fused_computation.95 | convolution fusion | flops 17104384 | bytes 790528 | tf_op jit(solution)/shard_map/bthd,buhd->bhtu/dot_general | solution.py:73
  81.4 3.4 %collective-permute-start.19 = (bf16[256,256]{1,0:T(8,128)(2,1)}, bf16[256,256]{1,0:T(8,128)(2,1)}, u32[]{:S(2)}, u32[]{:S(2)}) collective-permute-start(bf16[256,256]{1,0:T(8,128)(2,1)} %fusion.31), channel_id=1, source_target_pairs={{1,0},{2,1},{3,2},{4,3},{5,4},{6,5},{7,6},{8,7},{9,8},{10,9},{11,1... | collective-permute-start | bytes 393224 | tf_op jit(solution)/shard_map/ppermute | solution.py:13
  86.5 3.2 %collective-permute-start.15 = (bf16[256,256]{1,0:T(8,128)(2,1)}, bf16[256,256]{1,0:T(8,128)(2,1)}, u32[]{:S(2)}, u32[]{:S(2)}) collective-permute-start(bf16[256,256]{1,0:T(8,128)(2,1)} %bitcast.165), channel_id=1, source_target_pairs={{2,0},{3,1},{4,2},{5,3},{6,4},{7,5},{8,6},{9,7},{10,8},{11,9},{12,... | collective-permute-start | bytes 393224 | tf_op jit(solution)/shard_map/ppermute | solution.py:13
  90.5 8.1 %collective-permute-start.16 = (bf16[256,256]{1,0:T(8,128)(2,1)}, bf16[256,256]{1,0:T(8,128)(2,1)}, u32[]{:S(2)}, u32[]{:S(2)}) collective-permute-start(bf16[256,256]{1,0:T(8,128)(2,1)} %bitcast.164), channel_id=1, source_target_pairs={{4,0},{5,1},{6,2},{7,3},{8,4},{9,5},{10,6},{11,7},{12,8},{13,9},{1... | collective-permute-start | bytes 393224 | tf_op jit(solution)/shard_map/ppermute | solution.py:13
  99.5 2.0 %collective-permute-start.17 = (bf16[256,256]{1,0:T(8,128)(2,1)}, bf16[256,256]{1,0:T(8,128)(2,1)}, u32[]{:S(2)}, u32[]{:S(2)}) collective-permute-start(bf16[256,256]{1,0:T(8,128)(2,1)} %bitcast.163), channel_id=1, source_target_pairs={{8,0},{9,1},{10,2},{11,3},{12,4},{13,5},{14,6},{15,7},{16,8},{17,9... | collective-permute-start | bytes 393224 | tf_op jit(solution)/shard_map/ppermute | solution.py:13
  112.9 8.9 %collective-permute-start.14 = (bf16[256,256]{1,0:T(8,128)(2,1)S(1)}, bf16[256,256]{1,0:T(8,128)(2,1)S(1)}, u32[]{:S(2)}, u32[]{:S(2)}) collective-permute-start(bf16[256,256]{1,0:T(8,128)(2,1)S(1)} %fusion.38), channel_id=1, source_target_pairs={{1,0},{2,1},{3,2},{4,3},{5,4},{6,5},{7,6},{8,7},{9,8},{10,9},{11,1... | collective-permute-start | bytes 393224 | tf_op jit(solution)/shard_map/ppermute | solution.py:13
  121.8 1.9 %collective-permute-start.10 = (bf16[256,256]{1,0:T(8,128)(2,1)S(1)}, bf16[256,256]{1,0:T(8,128)(2,1)S(1)}, u32[]{:S(2)}, u32[]{:S(2)}) collective-permute-start(bf16[256,256]{1,0:T(8,128)(2,1)S(1)} %bitcast.189), channel_id=1, source_target_pairs={{2,0},{3,1},{4,2},{5,3},{6,4},{7,5},{8,6},{9,7},{10,8},{11,9},{12,... | collective-permute-start | bytes 393224 | tf_op jit(solution)/shard_map/ppermute | solution.py:13
  123.7 5.3 %collective-permute-start.11 = (bf16[256,256]{1,0:T(8,128)(2,1)S(1)}, bf16[256,256]{1,0:T(8,128)(2,1)S(1)}, u32[]{:S(2)}, u32[]{:S(2)}) collective-permute-start(bf16[256,256]{1,0:T(8,128)(2,1)S(1)} %bitcast.190), channel_id=1, source_target_pairs={{4,0},{5,1},{6,2},{7,3},{8,4},{9,5},{10,6},{11,7},{12,8},{13,9},{1... | collective-permute-start | bytes 393224 | tf_op jit(solution)/shard_map/ppermute | solution.py:13
  129.1 1.9 %collective-permute-start.12 = (bf16[256,256]{1,0:T(8,128)(2,1)S(1)}, bf16[256,256]{1,0:T(8,128)(2,1)S(1)}, u32[]{:S(2)}, u32[]{:S(2)}) collective-permute-start(bf16[256,256]{1,0:T(8,128)(2,1)S(1)} %bitcast.191), channel_id=1, source_target_pairs={{8,0},{9,1},{10,2},{11,3},{12,4},{13,5},{14,6},{15,7},{16,8},{17,9... | collective-permute-start | bytes 393224 | tf_op jit(solution)/shard_map/ppermute | solution.py:13
  132.3 1.9 %fusion.37 = bf16[256,256]{1,0:T(8,128)(2,1)} fusion(f32[32,8,2,128]{3,2,1,0:T(2,128)S(1)} %bitcast.173, bf16[256,256]{1,0:T(8,128)(2,1)} %collective-permute-done.19, bf16[256,256]{1,0:T(8,128)(2,1)} %collective-permute-done.18, bf16[256,256]{1,0:T(8,128)(2,1)} %collective-permute-done.17, bf16[256,256]{1,0:T(8,128)(2,1)} %collective-permute-done.16, ...), kind=kLoop, calls=%fused_computation.68 | loop fusion | flops 786432 | bytes 1179648 | tf_op jit(solution)/shard_map/convert_element_type | solution.py:138
  134.3 3.6 %collective-permute-done.12 = bf16[256,256]{1,0:T(8,128)(2,1)S(1)} collective-permute-done((bf16[256,256]{1,0:T(8,128)(2,1)S(1)}, bf16[256,256]{1,0:T(8,128)(2,1)S(1)}, u32[]{:S(2)}, u32[]{:S(2)}) %collective-permute-start.12) | collective-permute-done | bytes 131104 | tf_op jit(solution)/shard_map/ppermute | solution.py:13
  137.9 1.9 %collective-permute-done.13 = bf16[256,256]{1,0:T(8,128)(2,1)S(1)} collective-permute-done((bf16[256,256]{1,0:T(8,128)(2,1)S(1)}, bf16[256,256]{1,0:T(8,128)(2,1)S(1)}, u32[]{:S(2)}, u32[]{:S(2)}) %collective-permute-start.13) | collective-permute-done | bytes 131104 | tf_op jit(solution)/shard_map/ppermute | solution.py:13
  (185 shorter events, 44.3 us)
Async XLA Ops:
  0.6 32.0 %collective-permute-start = (bf16[256,256]{1,0:T(8,128)(2,1)}, bf16[256,256]{1,0:T(8,128)(2,1)S(1)}, u32[]{:S(2)}, u32[]{:S(2)}) collective-permute-start(bf16[256,256]{1,0:T(8,128)(2,1)} %param.7), channel_id=1, source_target_pairs={{0,1},{1,2},{2,3},{3,4},{4,5},{5,6},{6,7},{7,8},{8,9},{9,10},{10,1... | collective-permute-start | bytes 393224 | tf_op jit(solution)/shard_map/ppermute | solution.py:13
  15.5 25.7 %collective-permute-start.4 = (bf16[256,256]{1,0:T(8,128)(2,1)}, bf16[256,256]{1,0:T(8,128)(2,1)S(1)}, u32[]{:S(2)}, u32[]{:S(2)}) collective-permute-start(bf16[256,256]{1,0:T(8,128)(2,1)} %param.7), channel_id=1, source_target_pairs={{0,16},{1,17},{2,18},{3,19},{4,20},{5,21},{6,22},{7,23},{8,24},{9,... | collective-permute-start | bytes 393224 | tf_op jit(solution)/shard_map/ppermute | solution.py:13
  19.7 26.3 %collective-permute-start.3 = (bf16[256,256]{1,0:T(8,128)(2,1)}, bf16[256,256]{1,0:T(8,128)(2,1)S(1)}, u32[]{:S(2)}, u32[]{:S(2)}) collective-permute-start(bf16[256,256]{1,0:T(8,128)(2,1)} %param.7), channel_id=1, source_target_pairs={{0,8},{1,9},{2,10},{3,11},{4,12},{5,13},{6,14},{7,15},{8,16},{9,17... | collective-permute-start | bytes 393224 | tf_op jit(solution)/shard_map/ppermute | solution.py:13
  21.6 27.0 %collective-permute-start.2 = (bf16[256,256]{1,0:T(8,128)(2,1)}, bf16[256,256]{1,0:T(8,128)(2,1)S(1)}, u32[]{:S(2)}, u32[]{:S(2)}) collective-permute-start(bf16[256,256]{1,0:T(8,128)(2,1)} %param.7), channel_id=1, source_target_pairs={{0,4},{1,5},{2,6},{3,7},{4,8},{5,9},{6,10},{7,11},{8,12},{9,13},{1... | collective-permute-start | bytes 393224 | tf_op jit(solution)/shard_map/ppermute | solution.py:13
  24.3 27.8 %collective-permute-start.1 = (bf16[256,256]{1,0:T(8,128)(2,1)}, bf16[256,256]{1,0:T(8,128)(2,1)S(1)}, u32[]{:S(2)}, u32[]{:S(2)}) collective-permute-start(bf16[256,256]{1,0:T(8,128)(2,1)} %param.7), channel_id=1, source_target_pairs={{0,2},{1,3},{2,4},{3,5},{4,6},{5,7},{6,8},{7,9},{8,10},{9,11},{10,... | collective-permute-start | bytes 393224 | tf_op jit(solution)/shard_map/ppermute | solution.py:13
  32.7 30.4 %collective-permute-start.5 = (bf16[256,256]{1,0:T(8,128)(2,1)S(1)}, bf16[256,256]{1,0:T(8,128)(2,1)S(1)}, u32[]{:S(2)}, u32[]{:S(2)}) collective-permute-start(bf16[256,256]{1,0:T(8,128)(2,1)S(1)} %copy-done.6), channel_id=1, source_target_pairs={{0,1},{1,2},{2,3},{3,4},{4,5},{5,6},{6,7},{7,8},{8,9},{9,10},{10,1... | collective-permute-start | bytes 393224 | tf_op jit(solution)/shard_map/ppermute | solution.py:13
  41.2 22.8 %collective-permute-start.9 = (bf16[256,256]{1,0:T(8,128)(2,1)S(1)}, bf16[256,256]{1,0:T(8,128)(2,1)S(1)}, u32[]{:S(2)}, u32[]{:S(2)}) collective-permute-start(bf16[256,256]{1,0:T(8,128)(2,1)S(1)} %copy-done.6), channel_id=1, source_target_pairs={{0,16},{1,17},{2,18},{3,19},{4,20},{5,21},{6,22},{7,23},{8,24},{9,... | collective-permute-start | bytes 393224 | tf_op jit(solution)/shard_map/ppermute | solution.py:13
  46.0 18.2 %collective-permute-start.8 = (bf16[256,256]{1,0:T(8,128)(2,1)S(1)}, bf16[256,256]{1,0:T(8,128)(2,1)S(1)}, u32[]{:S(2)}, u32[]{:S(2)}) collective-permute-start(bf16[256,256]{1,0:T(8,128)(2,1)S(1)} %copy-done.6), channel_id=1, source_target_pairs={{0,8},{1,9},{2,10},{3,11},{4,12},{5,13},{6,14},{7,15},{8,16},{9,17... | collective-permute-start | bytes 393224 | tf_op jit(solution)/shard_map/ppermute | solution.py:13
  48.6 15.9 %collective-permute-start.7 = (bf16[256,256]{1,0:T(8,128)(2,1)S(1)}, bf16[256,256]{1,0:T(8,128)(2,1)S(1)}, u32[]{:S(2)}, u32[]{:S(2)}) collective-permute-start(bf16[256,256]{1,0:T(8,128)(2,1)S(1)} %copy-done.6), channel_id=1, source_target_pairs={{0,4},{1,5},{2,6},{3,7},{4,8},{5,9},{6,10},{7,11},{8,12},{9,13},{1... | collective-permute-start | bytes 393224 | tf_op jit(solution)/shard_map/ppermute | solution.py:13
  52.1 12.7 %collective-permute-start.6 = (bf16[256,256]{1,0:T(8,128)(2,1)S(1)}, bf16[256,256]{1,0:T(8,128)(2,1)}, u32[]{:S(2)}, u32[]{:S(2)}) collective-permute-start(bf16[256,256]{1,0:T(8,128)(2,1)S(1)} %copy-done.6), channel_id=1, source_target_pairs={{0,2},{1,3},{2,4},{3,5},{4,6},{5,7},{6,8},{7,9},{8,10},{9,11},{10,... | collective-permute-start | bytes 393224 | tf_op jit(solution)/shard_map/ppermute | solution.py:13
  81.4 31.5 %collective-permute-start.19 = (bf16[256,256]{1,0:T(8,128)(2,1)}, bf16[256,256]{1,0:T(8,128)(2,1)}, u32[]{:S(2)}, u32[]{:S(2)}) collective-permute-start(bf16[256,256]{1,0:T(8,128)(2,1)} %fusion.31), channel_id=1, source_target_pairs={{1,0},{2,1},{3,2},{4,3},{5,4},{6,5},{7,6},{8,7},{9,8},{10,9},{11,1... | collective-permute-start | bytes 393224 | tf_op jit(solution)/shard_map/ppermute | solution.py:13
  86.5 35.2 %collective-permute-start.15 = (bf16[256,256]{1,0:T(8,128)(2,1)}, bf16[256,256]{1,0:T(8,128)(2,1)}, u32[]{:S(2)}, u32[]{:S(2)}) collective-permute-start(bf16[256,256]{1,0:T(8,128)(2,1)} %bitcast.165), channel_id=1, source_target_pairs={{2,0},{3,1},{4,2},{5,3},{6,4},{7,5},{8,6},{9,7},{10,8},{11,9},{12,... | collective-permute-start | bytes 393224 | tf_op jit(solution)/shard_map/ppermute | solution.py:13
  90.5 33.2 %collective-permute-start.16 = (bf16[256,256]{1,0:T(8,128)(2,1)}, bf16[256,256]{1,0:T(8,128)(2,1)}, u32[]{:S(2)}, u32[]{:S(2)}) collective-permute-start(bf16[256,256]{1,0:T(8,128)(2,1)} %bitcast.164), channel_id=1, source_target_pairs={{4,0},{5,1},{6,2},{7,3},{8,4},{9,5},{10,6},{11,7},{12,8},{13,9},{1... | collective-permute-start | bytes 393224 | tf_op jit(solution)/shard_map/ppermute | solution.py:13
  99.5 29.6 %collective-permute-start.17 = (bf16[256,256]{1,0:T(8,128)(2,1)}, bf16[256,256]{1,0:T(8,128)(2,1)}, u32[]{:S(2)}, u32[]{:S(2)}) collective-permute-start(bf16[256,256]{1,0:T(8,128)(2,1)} %bitcast.163), channel_id=1, source_target_pairs={{8,0},{9,1},{10,2},{11,3},{12,4},{13,5},{14,6},{15,7},{16,8},{17,9... | collective-permute-start | bytes 393224 | tf_op jit(solution)/shard_map/ppermute | solution.py:13
  102.3 28.7 %collective-permute-start.18 = (bf16[256,256]{1,0:T(8,128)(2,1)}, bf16[256,256]{1,0:T(8,128)(2,1)}, u32[]{:S(2)}, u32[]{:S(2)}) collective-permute-start(bf16[256,256]{1,0:T(8,128)(2,1)} %bitcast.162), channel_id=1, source_target_pairs={{16,0},{17,1},{18,2},{19,3},{20,4},{21,5},{22,6},{23,7},{24,8},{25... | collective-permute-start | bytes 393224 | tf_op jit(solution)/shard_map/ppermute | solution.py:13
  112.8 8.9 %copy-start.30 = (bf16[32,8,2,128]{3,1,2,0:T(8,128)(2,1)S(1)}, bf16[32,8,2,128]{3,1,2,0:T(8,128)(2,1)}, u32[]{:S(2)}) copy-start(bf16[32,8,2,128]{3,1,2,0:T(8,128)(2,1)} %copy.327) | copy-start | bytes 393220
  112.8 10.9 %copy-start.31 = (bf16[32,8,2,128]{3,1,2,0:T(8,128)(2,1)S(1)}, bf16[32,8,2,128]{3,1,2,0:T(8,128)(2,1)}, u32[]{:S(2)}) copy-start(bf16[32,8,2,128]{3,1,2,0:T(8,128)(2,1)} %copy.326) | copy-start | bytes 393220
  112.8 16.2 %copy-start.32 = (bf16[32,8,2,128]{3,1,2,0:T(8,128)(2,1)S(1)}, bf16[32,8,2,128]{3,1,2,0:T(8,128)(2,1)}, u32[]{:S(2)}) copy-start(bf16[32,8,2,128]{3,1,2,0:T(8,128)(2,1)} %copy.325) | copy-start | bytes 393220
  112.8 18.2 %copy-start.33 = (bf16[32,8,2,128]{3,1,2,0:T(8,128)(2,1)S(1)}, bf16[32,8,2,128]{3,1,2,0:T(8,128)(2,1)}, u32[]{:S(2)}) copy-start(bf16[32,8,2,128]{3,1,2,0:T(8,128)(2,1)} %copy.324) | copy-start | bytes 393220
  112.9 21.4 %collective-permute-start.14 = (bf16[256,256]{1,0:T(8,128)(2,1)S(1)}, bf16[256,256]{1,0:T(8,128)(2,1)S(1)}, u32[]{:S(2)}, u32[]{:S(2)}) collective-permute-start(bf16[256,256]{1,0:T(8,128)(2,1)S(1)} %fusion.38), channel_id=1, source_target_pairs={{1,0},{2,1},{3,2},{4,3},{5,4},{6,5},{7,6},{8,7},{9,8},{10,9},{11,1... | collective-permute-start | bytes 393224 | tf_op jit(solution)/shard_map/ppermute | solution.py:13
  121.8 12.5 %collective-permute-start.10 = (bf16[256,256]{1,0:T(8,128)(2,1)S(1)}, bf16[256,256]{1,0:T(8,128)(2,1)S(1)}, u32[]{:S(2)}, u32[]{:S(2)}) collective-permute-start(bf16[256,256]{1,0:T(8,128)(2,1)S(1)} %bitcast.189), channel_id=1, source_target_pairs={{2,0},{3,1},{4,2},{5,3},{6,4},{7,5},{8,6},{9,7},{10,8},{11,9},{12,... | collective-permute-start | bytes 393224 | tf_op jit(solution)/shard_map/ppermute | solution.py:13
  123.7 10.5 %collective-permute-start.11 = (bf16[256,256]{1,0:T(8,128)(2,1)S(1)}, bf16[256,256]{1,0:T(8,128)(2,1)S(1)}, u32[]{:S(2)}, u32[]{:S(2)}) collective-permute-start(bf16[256,256]{1,0:T(8,128)(2,1)S(1)} %bitcast.190), channel_id=1, source_target_pairs={{4,0},{5,1},{6,2},{7,3},{8,4},{9,5},{10,6},{11,7},{12,8},{13,9},{1... | collective-permute-start | bytes 393224 | tf_op jit(solution)/shard_map/ppermute | solution.py:13
  129.1 8.8 %collective-permute-start.12 = (bf16[256,256]{1,0:T(8,128)(2,1)S(1)}, bf16[256,256]{1,0:T(8,128)(2,1)S(1)}, u32[]{:S(2)}, u32[]{:S(2)}) collective-permute-start(bf16[256,256]{1,0:T(8,128)(2,1)S(1)} %bitcast.191), channel_id=1, source_target_pairs={{8,0},{9,1},{10,2},{11,3},{12,4},{13,5},{14,6},{15,7},{16,8},{17,9... | collective-permute-start | bytes 393224 | tf_op jit(solution)/shard_map/ppermute | solution.py:13
  131.0 8.8 %collective-permute-start.13 = (bf16[256,256]{1,0:T(8,128)(2,1)S(1)}, bf16[256,256]{1,0:T(8,128)(2,1)S(1)}, u32[]{:S(2)}, u32[]{:S(2)}) collective-permute-start(bf16[256,256]{1,0:T(8,128)(2,1)S(1)} %bitcast.192), channel_id=1, source_target_pairs={{16,0},{17,1},{18,2},{19,3},{20,4},{21,5},{22,6},{23,7},{24,8},{25... | collective-permute-start | bytes 393224 | tf_op jit(solution)/shard_map/ppermute | solution.py:13
  (32 other events, 54.8 us)
where the time goes:
time: 142 us; the launch traced here: 141 us
  starting transfers between devices  84.9 us (60%)
  local copies, waits for them, and re-layouts  26.4 us (19%)
  matrix products  15.9 us (11%)
  other arithmetic  6.19 us (4%)
  waiting for transfers between devices  5.6 us (4%)
  between operations  1.57 us (1%)
    ppermute x20, starting transfers between devices, from_behind(): lax.ppermute(value, axis, [(source, source + steps) for source in range(i...  84.9 us
    unnamed x81, local copies, waits for them, and re-layouts  17 us
    dot_general x7, matrix products, on_device(): jnp.einsum('bhtu,bthd->buhd', weights, g_blocks, preferred_element_type=j...  6.07 us
    ppermute x20, waiting for transfers between devices, from_behind(): lax.ppermute(value, axis, [(source, source + steps) for source in range(i...  5.6 us
    reshape x17, local copies, waits for them, and re-layouts, to_blocks(): return array.reshape(blocks_here, BLOCK, HEADS, head_size)  5.43 us
    dot_general x7, matrix products, on_device(): jnp.einsum('bthd,buhd->bhtu', g_blocks, to_blocks(level_values), preferre...  4.2 us
  transfers between devices with their start and end apart: 20, of which 2 were waited for; matrix products, arithmetic and copies ran while one was open for 17% of the time, Pallas kernels for 0%

commit v1 on v0

v1 whole, which is shorter than its diff:
```python
import jax
import jax.numpy as jnp
from jax import lax
from jax.sharding import PartitionSpec as P

BLOCK = 128
HEADS = 2


def from_behind(value, axis, steps):
    count = lax.axis_size(axis)
    initial, last = (max(0, -steps), min(count, count - steps))
    return lax.ppermute(value, axis, [(source, source + steps) for source in range(initial, last)])


def on_device(queries, keys, values, out_grad, block_list, causal):
    tok_rows, feat = queries.shape
    blocks_here = tok_rows // BLOCK
    entries = block_list.shape[1]
    head_size = feat // HEADS
    scale = head_size ** (-0.5)
    far_levels = [level for level in range(1, entries) if 2 ** (level - 1) > blocks_here]
    near_levels = [level for level in range(1, entries) if 2 ** (level - 1) <= blocks_here]

    def to_blocks(array):
        return array.reshape(array.shape[:-2] + (blocks_here, BLOCK, HEADS, head_size))

    kv_own = jnp.concatenate([keys, values], 1)
    qg_own = jnp.concatenate([queries, out_grad], 1)
    kv_near = from_behind(kv_own, "ctx", 1)
    qg_next = from_behind(qg_own, "ctx", -1)
    kv_far = {}
    qg_far = {}
    for level in far_levels:
        distance = 2 ** (level - 1) // blocks_here
        kv_far[level] = from_behind(kv_own, "ctx", distance)
        qg_far[level] = from_behind(qg_own, "ctx", -distance)

    kv_joined = jnp.concatenate([kv_near, kv_own], 0)
    kv_levels = []
    for level in range(entries):
        if level == 0:
            kv_levels.append(kv_own)
        elif level in near_levels:
            start = (blocks_here - 2 ** (level - 1)) * BLOCK
            kv_levels.append(kv_joined[start : start + tok_rows])
        else:
            kv_levels.append(kv_far[level])
    kv_stack = jnp.stack(kv_levels, 0)
    k_stack = to_blocks(kv_stack[..., :feat])
    v_stack = to_blocks(kv_stack[..., feat:])
    q_blocks = to_blocks(queries)
    g_blocks = to_blocks(out_grad)

    positions = jnp.arange(BLOCK)
    lower = positions[:, None] >= positions[None, :]
    valid = block_list >= 0
    self_mask = jnp.where(causal[:, None, None] > 0, lower[None], True) & valid[:, 0, None, None]
    level_mask = jnp.concatenate(
        [self_mask[None], jnp.broadcast_to(valid.T[1:, :, None, None], (entries - 1, blocks_here, BLOCK, BLOCK))], 0
    )

    scores = jnp.einsum("bthd,lbuhd->lbhtu", q_blocks, k_stack, preferred_element_type=jnp.float32) * scale
    scores = jnp.where(level_mask[:, :, None], scores, -jnp.inf)
    top = scores.max(axis=(0, 4))
    lse = top + jnp.log(jnp.sum(jnp.exp(scores - top[None, ..., None]), axis=(0, 4)))
    probs = jnp.exp(scores - lse[None, ..., None])
    weights = probs.astype(jnp.bfloat16)
    dprobs = jnp.einsum("bthd,lbuhd->lbhtu", g_blocks, v_stack, preferred_element_type=jnp.float32)
    delta = jnp.sum(weights.astype(jnp.float32) * dprobs, axis=(0, 4))
    dscores = (probs * (dprobs - delta[None, ..., None])).astype(jnp.bfloat16)
    query_grad = jnp.einsum("lbhtu,lbuhd->bthd", dscores, k_stack, preferred_element_type=jnp.float32) * scale
    key_grad = jnp.einsum("bhtu,bthd->buhd", dscores[0], q_blocks, preferred_element_type=jnp.float32) * scale
    value_grad = jnp.einsum("bhtu,bthd->buhd", weights[0], g_blocks, preferred_element_type=jnp.float32)

    masked_lse = jnp.where(valid.T[:, :, None, None], lse[None], jnp.inf)
    stats_own = {level: jnp.stack([masked_lse[level], delta], 0) for level in range(1, entries)}
    near_stats = jnp.stack([stats_own[level] for level in near_levels], 0)
    near_back = from_behind(near_stats, "ctx", -1)
    stats_next = {level: near_back[index] for index, level in enumerate(near_levels)}
    far_back = {}
    for level in far_levels:
        distance = 2 ** (level - 1) // blocks_here
        far_back[level] = from_behind(stats_own[level], "ctx", -distance)

    qg_joined = jnp.concatenate([qg_own, qg_next], 0)
    qg_levels = []
    stat_levels = []
    for level in range(1, entries):
        reach = 2 ** (level - 1)
        if level in near_levels:
            start = reach * BLOCK
            qg_levels.append(qg_joined[start : start + tok_rows])
            joined_stats = jnp.concatenate([stats_own[level], stats_next[level]], 1)
            stat_levels.append(joined_stats[:, reach : reach + blocks_here])
        else:
            qg_levels.append(qg_far[level])
            stat_levels.append(far_back[level])
    qg_stack = jnp.stack(qg_levels, 0)
    stat_stack = jnp.stack(stat_levels, 0)
    qk_stack = to_blocks(qg_stack[..., :feat])
    gk_stack = to_blocks(qg_stack[..., feat:])
    k_blocks = to_blocks(keys)
    v_blocks = to_blocks(values)
    other_scores = jnp.einsum("lbthd,buhd->lbhtu", qk_stack, k_blocks, preferred_element_type=jnp.float32) * scale
    other_probs = jnp.exp(other_scores - stat_stack[:, 0, ..., None])
    other_weights = other_probs.astype(jnp.bfloat16)
    other_dprobs = jnp.einsum("lbthd,buhd->lbhtu", gk_stack, v_blocks, preferred_element_type=jnp.float32)
    other_dscores = (other_probs * (other_dprobs - stat_stack[:, 1, ..., None])).astype(jnp.bfloat16)
    key_grad = key_grad + jnp.einsum(
        "lbhtu,lbthd->buhd", other_dscores, qk_stack, preferred_element_type=jnp.float32
    ) * scale
    value_grad = value_grad + jnp.einsum(
        "lbhtu,lbthd->buhd", other_weights, gk_stack, preferred_element_type=jnp.float32
    )
    return (
        query_grad.astype(jnp.bfloat16).reshape(tok_rows, feat),
        key_grad.astype(jnp.bfloat16).reshape(tok_rows, feat),
        value_grad.astype(jnp.bfloat16).reshape(tok_rows, feat),
    )


def solution(mesh):
    return jax.shard_map(
        on_device,
        mesh=mesh,
        in_specs=(
            P(("dp", "ctx"), None),
            P(("dp", "ctx"), None),
            P(("dp", "ctx"), None),
            P(("dp", "ctx"), None),
            P(("dp", "ctx"), None),
            P(("dp", "ctx")),
        ),
        out_specs=(P(("dp", "ctx"), None), P(("dp", "ctx"), None), P(("dp", "ctx"), None)),
        check_vma=False,
    )
```

time: 142 us -> 128 us (0.901)
  the two profiles are of different devices: /device:TPU:46 before, /device:TPU:206 now
where the time goes in v1:
time: 128 us; the launch traced here: 127 us
  starting transfers between devices  65.4 us (51%)
  local copies, waits for them, and re-layouts  28.5 us (22%)
  waiting for transfers between devices  19.9 us (16%)
  matrix products  7.78 us (6%)
  other arithmetic  4.55 us (4%)
    ppermute x15, starting transfers between devices, from_behind(): lax.ppermute(value, axis, [(source, source + steps) for source in range(i...  65.4 us
    ppermute x15, waiting for transfers between devices, from_behind(): lax.ppermute(value, axis, [(source, source + steps) for source in range(i...  19.9 us
    unnamed x40, local copies, waits for them, and re-layouts  9.58 us
    reshape x11, local copies, waits for them, and re-layouts, to_blocks(): array.reshape(array.shape[:-2] + (blocks_here, BLOCK, HEADS, head_size))  8.1 us
  transfers between devices with their start and end apart: 15, of which 4 were waited for; matrix products, arithmetic and copies ran while one was open for 19% of the time, Pallas kernels for 0%

profile of v1, /device:TPU:206, one launch (start us, length us, event | category | flops | bytes accessed | tf_op | source)
XLA Modules:
  0.0 127.3 jit_solution(124640604401229546)
XLA Ops:
  2.6 9.1 %collective-permute-start = (bf16[256,512]{1,0:T(8,128)(2,1)S(1)}, bf16[256,512]{1,0:T(8,128)(2,1)S(1)}, u32[]{:S(2)}, u32[]{:S(2)}) collective-permute-start(bf16[256,512]{1,0:T(8,128)(2,1)S(1)} %constant_dynamic-update-slice_fusion), channel_id=1, source_target_pairs={{0,1},{1,2},{2,3},{3,4},{4,5},{5,6},{6,7},{7,8},{8,9},{9,10},{10,1... | collective-permute-start | bytes 786440 | tf_op jit(solution)/shard_map/ppermute | solution.py:13
  11.7 3.4 %collective-permute-start.1 = (bf16[256,512]{1,0:T(8,128)(2,1)S(1)}, bf16[256,512]{1,0:T(8,128)(2,1)S(1)}, u32[]{:S(2)}, u32[]{:S(2)}) collective-permute-start(bf16[256,512]{1,0:T(8,128)(2,1)S(1)} %constant_dynamic-update-slice_fusion), channel_id=1, source_target_pairs={{0,2},{1,3},{2,4},{3,5},{4,6},{5,7},{6,8},{7,9},{8,10},{9,11},{10,... | collective-permute-start | bytes 786440 | tf_op jit(solution)/shard_map/ppermute | solution.py:13
  15.1 4.3 %collective-permute-start.2 = (bf16[256,512]{1,0:T(8,128)(2,1)S(1)}, bf16[256,512]{1,0:T(8,128)(2,1)S(1)}, u32[]{:S(2)}, u32[]{:S(2)}) collective-permute-start(bf16[256,512]{1,0:T(8,128)(2,1)S(1)} %constant_dynamic-update-slice_fusion), channel_id=1, source_target_pairs={{0,4},{1,5},{2,6},{3,7},{4,8},{5,9},{6,10},{7,11},{8,12},{9,13},{1... | collective-permute-start | bytes 786440 | tf_op jit(solution)/shard_map/ppermute | solution.py:13
  19.4 3.2 %collective-permute-start.3 = (bf16[256,512]{1,0:T(8,128)(2,1)S(1)}, bf16[256,512]{1,0:T(8,128)(2,1)S(1)}, u32[]{:S(2)}, u32[]{:S(2)}) collective-permute-start(bf16[256,512]{1,0:T(8,128)(2,1)S(1)} %constant_dynamic-update-slice_fusion), channel_id=1, source_target_pairs={{0,8},{1,9},{2,10},{3,11},{4,12},{5,13},{6,14},{7,15},{8,16},{9,17... | collective-permute-start | bytes 786440 | tf_op jit(solution)/shard_map/ppermute | solution.py:13
  31.9 6.4 %collective-permute-done = bf16[256,512]{1,0:T(8,128)(2,1)S(1)} collective-permute-done((bf16[256,512]{1,0:T(8,128)(2,1)S(1)}, bf16[256,512]{1,0:T(8,128)(2,1)S(1)}, u32[]{:S(2)}, u32[]{:S(2)}) %collective-permute-start) | collective-permute-done | bytes 262176 | tf_op jit(solution)/shard_map/ppermute | solution.py:13
  38.3 9.1 %collective-permute-start.5 = (bf16[256,512]{1,0:T(8,128)(2,1)}, bf16[256,512]{1,0:T(8,128)(2,1)S(1)}, u32[]{:S(2)}, u32[]{:S(2)}) collective-permute-start(bf16[256,512]{1,0:T(8,128)(2,1)} %constant_dynamic-update-slice_fusion.2), channel_id=1, source_target_pairs={{1,0},{2,1},{3,2},{4,3},{5,4},{6,5},{7,6},{8,7},{9,8},{10,9},{11,1... | collective-permute-start | bytes 786440 | tf_op jit(solution)/shard_map/ppermute | solution.py:13
  47.5 2.4 %collective-permute-start.6 = (bf16[256,512]{1,0:T(8,128)(2,1)}, bf16[256,512]{1,0:T(8,128)(2,1)}, u32[]{:S(2)}, u32[]{:S(2)}) collective-permute-start(bf16[256,512]{1,0:T(8,128)(2,1)} %constant_dynamic-update-slice_fusion.2), channel_id=1, source_target_pairs={{2,0},{3,1},{4,2},{5,3},{6,4},{7,5},{8,6},{9,7},{10,8},{11,9},{12,... | collective-permute-start | bytes 786440 | tf_op jit(solution)/shard_map/ppermute | solution.py:13
  50.0 5.2 %collective-permute-start.7 = (bf16[256,512]{1,0:T(8,128)(2,1)}, bf16[256,512]{1,0:T(8,128)(2,1)}, u32[]{:S(2)}, u32[]{:S(2)}) collective-permute-start(bf16[256,512]{1,0:T(8,128)(2,1)} %constant_dynamic-update-slice_fusion.2), channel_id=1, source_target_pairs={{4,0},{5,1},{6,2},{7,3},{8,4},{9,5},{10,6},{11,7},{12,8},{13,9},{1... | collective-permute-start | bytes 786440 | tf_op jit(solution)/shard_map/ppermute | solution.py:13
  55.2 1.9 %collective-permute-start.8 = (bf16[256,512]{1,0:T(8,128)(2,1)}, bf16[256,512]{1,0:T(8,128)(2,1)}, u32[]{:S(2)}, u32[]{:S(2)}) collective-permute-start(bf16[256,512]{1,0:T(8,128)(2,1)} %constant_dynamic-update-slice_fusion.2), channel_id=1, source_target_pairs={{8,0},{9,1},{10,2},{11,3},{12,4},{13,5},{14,6},{15,7},{16,8},{17,9... | collective-permute-start | bytes 786440 | tf_op jit(solution)/shard_map/ppermute | solution.py:13
  61.6 7.8 %collective-permute-done.5 = bf16[256,512]{1,0:T(8,128)(2,1)S(1)} collective-permute-done((bf16[256,512]{1,0:T(8,128)(2,1)}, bf16[256,512]{1,0:T(8,128)(2,1)S(1)}, u32[]{:S(2)}, u32[]{:S(2)}) %collective-permute-start.5) | collective-permute-done | bytes 262176 | tf_op jit(solution)/shard_map/ppermute | solution.py:13
  71.7 1.7 %bitcast_dynamic-update-slice_fusion.3 = bf16[6,256,512]{2,1,0:T(8,128)(2,1)} fusion(bf16[6,256,512]{2,1,0:T(8,128)(2,1)} %bitcast_dynamic-update-slice_fusion.4, bf16[256,512]{1,0:T(8,128)(2,1)} %collective-permute-done.6), kind=kLoop, calls=%fused_computation.44 | loop fusion | bytes 524288
  73.4 1.7 %bitcast_dynamic-update-slice_fusion.2 = bf16[6,256,512]{2,1,0:T(8,128)(2,1)} fusion(bf16[6,256,512]{2,1,0:T(8,128)(2,1)} %bitcast_dynamic-update-slice_fusion.3, bf16[256,512]{1,0:T(8,128)(2,1)} %collective-permute-done.7), kind=kLoop, calls=%fused_computation.43 | loop fusion | bytes 524288
  75.4 2.9 %reshape.81 = bf16[7,2,128,2,128]{4,3,2,1,0:T(2,128)(2,1)} reshape(bf16[7,256,256]{2,1,0:T(8,128)(2,1)} %get-tuple-element.5) | data formatting | bytes 1835008 | tf_op jit(solution)/shard_map/reshape | solution.py:26
  78.3 1.7 %bitcast_dynamic-update-slice_fusion.1 = bf16[6,256,512]{2,1,0:T(8,128)(2,1)} fusion(bf16[6,256,512]{2,1,0:T(8,128)(2,1)} %bitcast_dynamic-update-slice_fusion.2, bf16[256,512]{1,0:T(8,128)(2,1)} %collective-permute-done.8), kind=kLoop, calls=%fused_computation.42 | loop fusion | bytes 524288
  79.9 1.7 %bitcast_dynamic-update-slice_fusion = bf16[6,256,512]{2,1,0:T(8,128)(2,1)} fusion(bf16[6,256,512]{2,1,0:T(8,128)(2,1)} %bitcast_dynamic-update-slice_fusion.1, bf16[256,512]{1,0:T(8,128)(2,1)} %collective-permute-done.9), kind=kLoop, calls=%fused_computation.41 | loop fusion | bytes 524288 | tf_op jit(solution)/shard_map/stack | solution.py:99
  81.7 2.4 %fusion.39 = (bf16[6,256,256]{2,1,0:T(8,128)(2,1)}, bf16[6,256,256]{2,1,0:T(8,128)(2,1)S(1)}) fusion(bf16[6,256,512]{2,1,0:T(8,128)(2,1)} %bitcast_dynamic-update-slice_fusion), kind=kLoop, calls=%fused_computation.96 | loop fusion | bytes 3145728 | tf_op jit(solution)/shard_map/slice | solution.py:102
  86.1 4.6 %collective-permute-start.10 = (f32[2,2,2,2,128]{4,3,2,1,0:T(2,128)S(1)}, f32[2,2,2,2,128]{4,3,2,1,0:T(2,128)S(1)}, u32[]{:S(2)}, u32[]{:S(2)}) collective-permute-start(f32[2,2,2,2,128]{4,3,2,1,0:T(2,128)S(1)} %pad_maximum_fusion.2), channel_id=1, source_target_pairs={{1,0},{2,1},{3,2},{4,3},{5,4},{6,5},{7,6},{8,7},{9,8},{10,9},{11,1... | collective-permute-start | bytes 24584 | tf_op jit(solution)/shard_map/ppermute | solution.py:13
  93.6 4.8 %collective-permute-start.11 = (f32[2,2,2,128]{3,2,1,0:T(2,128)S(1)}, f32[2,2,2,128]{3,2,1,0:T(2,128)S(1)}, u32[]{:S(2)}, u32[]{:S(2)}) collective-permute-start(f32[2,2,2,128]{3,2,1,0:T(2,128)S(1)} %get-tuple-element.19), channel_id=1, source_target_pairs={{2,0},{3,1},{4,2},{5,3},{6,4},{7,5},{8,6},{9,7},{10,8},{11,9},{12,... | collective-permute-start | bytes 12296 | tf_op jit(solution)/shard_map/ppermute | solution.py:13
  98.4 11.6 %collective-permute-start.12 = (f32[2,2,2,128]{3,2,1,0:T(2,128)S(1)}, f32[2,2,2,128]{3,2,1,0:T(2,128)S(1)}, u32[]{:S(2)}, u32[]{:S(2)}) collective-permute-start(f32[2,2,2,128]{3,2,1,0:T(2,128)S(1)} %get-tuple-element.20), channel_id=1, source_target_pairs={{4,0},{5,1},{6,2},{7,3},{8,4},{9,5},{10,6},{11,7},{12,8},{13,9},{1... | collective-permute-start | bytes 12296 | tf_op jit(solution)/shard_map/ppermute | solution.py:13
  110.0 1.9 %collective-permute-start.13 = (f32[2,2,2,128]{3,2,1,0:T(2,128)S(1)}, f32[2,2,2,128]{3,2,1,0:T(2,128)S(1)}, u32[]{:S(2)}, u32[]{:S(2)}) collective-permute-start(f32[2,2,2,128]{3,2,1,0:T(2,128)S(1)} %get-tuple-element.21), channel_id=1, source_target_pairs={{8,0},{9,1},{10,2},{11,3},{12,4},{13,5},{14,6},{15,7},{16,8},{17,9... | collective-permute-start | bytes 12296 | tf_op jit(solution)/shard_map/ppermute | solution.py:13
  113.3 2.2 %collective-permute-done.13 = f32[2,2,2,128]{3,2,1,0:T(2,128)S(1)} collective-permute-done((f32[2,2,2,128]{3,2,1,0:T(2,128)S(1)}, f32[2,2,2,128]{3,2,1,0:T(2,128)S(1)}, u32[]{:S(2)}, u32[]{:S(2)}) %collective-permute-start.13) | collective-permute-done | bytes 4128 | tf_op jit(solution)/shard_map/ppermute | solution.py:13
  115.5 3.4 %collective-permute-done.14 = f32[2,2,2,128]{3,2,1,0:T(2,128)S(1)} collective-permute-done((f32[2,2,2,128]{3,2,1,0:T(2,128)S(1)}, f32[2,2,2,128]{3,2,1,0:T(2,128)S(1)}, u32[]{:S(2)}, u32[]{:S(2)}) %collective-permute-start.14) | collective-permute-done | bytes 4128 | tf_op jit(solution)/shard_map/ppermute | solution.py:13
  122.6 1.8 %fusion.14 = f32[2,128,2,128]{1,3,2,0:T(8,128)S(1)} fusion(bf16[6,2,128,2,128]{2,4,0,3,1:T(8,128)(2,1)S(1)} %copy.38, f32[6,2,2,128,128]{4,3,0,2,1:T(8,128)S(1)} %fusion.6, bf16[6,2,128,2,128]{2,4,0,3,1:T(8,128)(2,1)S(1)} %copy.41, f32[6,2,2,128]{3,0,2,1:T(8,128)S(1)} %copy.37, bf16[2,128,2,128,1]{3,2,1,0,4:T(2,128)(2,1)} %reshape.94), kind=kOutput, calls=%fused_computation.25 | convolution fusion | flops 202571776 | bytes 3551232 | tf_op jit(solution)/shard_map/lbhtu,lbthd->buhd/dot_general | solution.py:110
  125.7 1.6 %copy_bitcast_fusion = (bf16[256,256]{1,0:T(8,128)(2,1)}, bf16[256,256]{1,0:T(8,128)(2,1)}) fusion(bf16[32,8,2,128]{3,2,1,0:T(2,128)(2,1)} %bitcast.153, bf16[32,8,2,128]{3,2,1,0:T(2,128)(2,1)S(1)} %bitcast.154), kind=kLoop, calls=%fused_computation.52 | loop fusion | bytes 524288 | tf_op jit(solution)/shard_map/reshape | solution.py:119
  (100 shorter events, 29.3 us)
Async XLA Ops:
  0.6 29.8 %copy-start.10 = (bf16[256,256]{1,0:T(8,128)(2,1)S(1)}, bf16[256,256]{1,0:T(8,128)(2,1)}, u32[]{:S(2)}) copy-start(bf16[256,256]{1,0:T(8,128)(2,1)} %param.7) | copy-start | bytes 393220
  0.6 30.5 %copy-start.11 = (bf16[256,256]{1,0:T(8,128)(2,1)S(1)}, bf16[256,256]{1,0:T(8,128)(2,1)}, u32[]{:S(2)}) copy-start(bf16[256,256]{1,0:T(8,128)(2,1)} %param.8) | copy-start | bytes 393220
  0.7 28.9 %copy-start.8 = (bf16[256,256]{1,0:T(8,128)(2,1)S(1)}, bf16[256,256]{1,0:T(8,128)(2,1)}, u32[]{:S(2)}) copy-start(bf16[256,256]{1,0:T(8,128)(2,1)} %param.6) | copy-start | bytes 393220
  0.7 29.0 %copy-start.9 = (bf16[256,256]{1,0:T(8,128)(2,1)S(1)}, bf16[256,256]{1,0:T(8,128)(2,1)}, u32[]{:S(2)}) copy-start(bf16[256,256]{1,0:T(8,128)(2,1)} %param.9) | copy-start | bytes 393220
  2.6 35.7 %collective-permute-start = (bf16[256,512]{1,0:T(8,128)(2,1)S(1)}, bf16[256,512]{1,0:T(8,128)(2,1)S(1)}, u32[]{:S(2)}, u32[]{:S(2)}) collective-permute-start(bf16[256,512]{1,0:T(8,128)(2,1)S(1)} %constant_dynamic-update-slice_fusion), channel_id=1, source_target_pairs={{0,1},{1,2},{2,3},{3,4},{4,5},{5,6},{6,7},{7,8},{8,9},{9,10},{10,1... | collective-permute-start | bytes 786440 | tf_op jit(solution)/shard_map/ppermute | solution.py:13
  11.7 35.8 %collective-permute-start.1 = (bf16[256,512]{1,0:T(8,128)(2,1)S(1)}, bf16[256,512]{1,0:T(8,128)(2,1)S(1)}, u32[]{:S(2)}, u32[]{:S(2)}) collective-permute-start(bf16[256,512]{1,0:T(8,128)(2,1)S(1)} %constant_dynamic-update-slice_fusion), channel_id=1, source_target_pairs={{0,2},{1,3},{2,4},{3,5},{4,6},{5,7},{6,8},{7,9},{8,10},{9,11},{10,... | collective-permute-start | bytes 786440 | tf_op jit(solution)/shard_map/ppermute | solution.py:13
  15.1 34.9 %collective-permute-start.2 = (bf16[256,512]{1,0:T(8,128)(2,1)S(1)}, bf16[256,512]{1,0:T(8,128)(2,1)S(1)}, u32[]{:S(2)}, u32[]{:S(2)}) collective-permute-start(bf16[256,512]{1,0:T(8,128)(2,1)S(1)} %constant_dynamic-update-slice_fusion), channel_id=1, source_target_pairs={{0,4},{1,5},{2,6},{3,7},{4,8},{5,9},{6,10},{7,11},{8,12},{9,13},{1... | collective-permute-start | bytes 786440 | tf_op jit(solution)/shard_map/ppermute | solution.py:13
  19.4 35.7 %collective-permute-start.3 = (bf16[256,512]{1,0:T(8,128)(2,1)S(1)}, bf16[256,512]{1,0:T(8,128)(2,1)S(1)}, u32[]{:S(2)}, u32[]{:S(2)}) collective-permute-start(bf16[256,512]{1,0:T(8,128)(2,1)S(1)} %constant_dynamic-update-slice_fusion), channel_id=1, source_target_pairs={{0,8},{1,9},{2,10},{3,11},{4,12},{5,13},{6,14},{7,15},{8,16},{9,17... | collective-permute-start | bytes 786440 | tf_op jit(solution)/shard_map/ppermute | solution.py:13
  22.6 34.5 %collective-permute-start.4 = (bf16[256,512]{1,0:T(8,128)(2,1)S(1)}, bf16[256,512]{1,0:T(8,128)(2,1)S(1)}, u32[]{:S(2)}, u32[]{:S(2)}) collective-permute-start(bf16[256,512]{1,0:T(8,128)(2,1)S(1)} %constant_dynamic-update-slice_fusion), channel_id=1, source_target_pairs={{0,16},{1,17},{2,18},{3,19},{4,20},{5,21},{6,22},{7,23},{8,24},{9,... | collective-permute-start | bytes 786440 | tf_op jit(solution)/shard_map/ppermute | solution.py:13
  29.6 31.4 %copy-start.5 = (bf16[2,128,2,128]{3,2,1,0:T(2,128)(2,1)}, bf16[2,128,2,128]{3,2,1,0:T(2,128)(2,1)S(1)}, u32[]{:S(2)}) copy-start(bf16[2,128,2,128]{3,2,1,0:T(2,128)(2,1)S(1)} %reshape.80) | copy-start | bytes 393220
  38.3 31.1 %collective-permute-start.5 = (bf16[256,512]{1,0:T(8,128)(2,1)}, bf16[256,512]{1,0:T(8,128)(2,1)S(1)}, u32[]{:S(2)}, u32[]{:S(2)}) collective-permute-start(bf16[256,512]{1,0:T(8,128)(2,1)} %constant_dynamic-update-slice_fusion.2), channel_id=1, source_target_pairs={{1,0},{2,1},{3,2},{4,3},{5,4},{6,5},{7,6},{8,7},{9,8},{10,9},{11,1... | collective-permute-start | bytes 786440 | tf_op jit(solution)/shard_map/ppermute | solution.py:13
  47.5 24.2 %collective-permute-start.6 = (bf16[256,512]{1,0:T(8,128)(2,1)}, bf16[256,512]{1,0:T(8,128)(2,1)}, u32[]{:S(2)}, u32[]{:S(2)}) collective-permute-start(bf16[256,512]{1,0:T(8,128)(2,1)} %constant_dynamic-update-slice_fusion.2), channel_id=1, source_target_pairs={{2,0},{3,1},{4,2},{5,3},{6,4},{7,5},{8,6},{9,7},{10,8},{11,9},{12,... | collective-permute-start | bytes 786440 | tf_op jit(solution)/shard_map/ppermute | solution.py:13
  50.0 23.4 %collective-permute-start.7 = (bf16[256,512]{1,0:T(8,128)(2,1)}, bf16[256,512]{1,0:T(8,128)(2,1)}, u32[]{:S(2)}, u32[]{:S(2)}) collective-permute-start(bf16[256,512]{1,0:T(8,128)(2,1)} %constant_dynamic-update-slice_fusion.2), channel_id=1, source_target_pairs={{4,0},{5,1},{6,2},{7,3},{8,4},{9,5},{10,6},{11,7},{12,8},{13,9},{1... | collective-permute-start | bytes 786440 | tf_op jit(solution)/shard_map/ppermute | solution.py:13
  55.2 23.1 %collective-permute-start.8 = (bf16[256,512]{1,0:T(8,128)(2,1)}, bf16[256,512]{1,0:T(8,128)(2,1)}, u32[]{:S(2)}, u32[]{:S(2)}) collective-permute-start(bf16[256,512]{1,0:T(8,128)(2,1)} %constant_dynamic-update-slice_fusion.2), channel_id=1, source_target_pairs={{8,0},{9,1},{10,2},{11,3},{12,4},{13,5},{14,6},{15,7},{16,8},{17,9... | collective-permute-start | bytes 786440 | tf_op jit(solution)/shard_map/ppermute | solution.py:13
  57.2 22.8 %collective-permute-start.9 = (bf16[256,512]{1,0:T(8,128)(2,1)}, bf16[256,512]{1,0:T(8,128)(2,1)}, u32[]{:S(2)}, u32[]{:S(2)}) collective-permute-start(bf16[256,512]{1,0:T(8,128)(2,1)} %constant_dynamic-update-slice_fusion.2), channel_id=1, source_target_pairs={{16,0},{17,1},{18,2},{19,3},{20,4},{21,5},{22,6},{23,7},{24,8},{25... | collective-permute-start | bytes 786440 | tf_op jit(solution)/shard_map/ppermute | solution.py:13
  79.9 4.2 %copy-start.3 = (bf16[2,128,2,128]{3,2,1,0:T(2,128)(2,1)S(1)}, bf16[2,128,2,128]{3,2,1,0:T(2,128)(2,1)}, u32[]{:S(2)}) copy-start(bf16[2,128,2,128]{3,2,1,0:T(2,128)(2,1)} %reshape.82) | copy-start | bytes 393220
  86.1 4.6 %copy-start = (bf16[7,2,2,128,128]{3,4,0,2,1:T(8,128)(2,1)}, bf16[7,2,2,128,128]{3,4,0,2,1:T(8,128)(2,1)S(1)}, u32[]{:S(2)}) copy-start(bf16[7,2,2,128,128]{3,4,0,2,1:T(8,128)(2,1)S(1)} %fusion.2) | copy-start | bytes 2752516
  86.1 5.9 %copy-start.2 = (bf16[6,256,256]{2,1,0:T(8,128)(2,1)S(1)}, bf16[6,256,256]{2,1,0:T(8,128)(2,1)}, u32[]{:S(2)}) copy-start(bf16[6,256,256]{2,1,0:T(8,128)(2,1)} %get-tuple-element.7) | copy-start | bytes 2359300
  86.1 27.1 %collective-permute-start.10 = (f32[2,2,2,2,128]{4,3,2,1,0:T(2,128)S(1)}, f32[2,2,2,2,128]{4,3,2,1,0:T(2,128)S(1)}, u32[]{:S(2)}, u32[]{:S(2)}) collective-permute-start(f32[2,2,2,2,128]{4,3,2,1,0:T(2,128)S(1)} %pad_maximum_fusion.2), channel_id=1, source_target_pairs={{1,0},{2,1},{3,2},{4,3},{5,4},{6,5},{7,6},{8,7},{9,8},{10,9},{11,1... | collective-permute-start | bytes 24584 | tf_op jit(solution)/shard_map/ppermute | solution.py:13
  92.8 26.2 %copy-start.7 = (bf16[2,128,2,128]{3,2,1,0:T(2,128)(2,1)S(1)}, bf16[2,128,2,128]{3,2,1,0:T(2,128)(2,1)}, u32[]{:S(2)}) copy-start(bf16[2,128,2,128]{3,2,1,0:T(2,128)(2,1)} %reshape.85) | copy-start | bytes 393220
  93.6 19.6 %collective-permute-start.11 = (f32[2,2,2,128]{3,2,1,0:T(2,128)S(1)}, f32[2,2,2,128]{3,2,1,0:T(2,128)S(1)}, u32[]{:S(2)}, u32[]{:S(2)}) collective-permute-start(f32[2,2,2,128]{3,2,1,0:T(2,128)S(1)} %get-tuple-element.19), channel_id=1, source_target_pairs={{2,0},{3,1},{4,2},{5,3},{6,4},{7,5},{8,6},{9,7},{10,8},{11,9},{12,... | collective-permute-start | bytes 12296 | tf_op jit(solution)/shard_map/ppermute | solution.py:13
  98.4 14.9 %collective-permute-start.12 = (f32[2,2,2,128]{3,2,1,0:T(2,128)S(1)}, f32[2,2,2,128]{3,2,1,0:T(2,128)S(1)}, u32[]{:S(2)}, u32[]{:S(2)}) collective-permute-start(f32[2,2,2,128]{3,2,1,0:T(2,128)S(1)} %get-tuple-element.20), channel_id=1, source_target_pairs={{4,0},{5,1},{6,2},{7,3},{8,4},{9,5},{10,6},{11,7},{12,8},{13,9},{1... | collective-permute-start | bytes 12296 | tf_op jit(solution)/shard_map/ppermute | solution.py:13
  110.0 5.5 %collective-permute-start.13 = (f32[2,2,2,128]{3,2,1,0:T(2,128)S(1)}, f32[2,2,2,128]{3,2,1,0:T(2,128)S(1)}, u32[]{:S(2)}, u32[]{:S(2)}) collective-permute-start(f32[2,2,2,128]{3,2,1,0:T(2,128)S(1)} %get-tuple-element.21), channel_id=1, source_target_pairs={{8,0},{9,1},{10,2},{11,3},{12,4},{13,5},{14,6},{15,7},{16,8},{17,9... | collective-permute-start | bytes 12296 | tf_op jit(solution)/shard_map/ppermute | solution.py:13
  111.9 7.0 %collective-permute-start.14 = (f32[2,2,2,128]{3,2,1,0:T(2,128)S(1)}, f32[2,2,2,128]{3,2,1,0:T(2,128)S(1)}, u32[]{:S(2)}, u32[]{:S(2)}) collective-permute-start(f32[2,2,2,128]{3,2,1,0:T(2,128)S(1)} %get-tuple-element.17), channel_id=1, source_target_pairs={{16,0},{17,1},{18,2},{19,3},{20,4},{21,5},{22,6},{23,7},{24,8},{25... | collective-permute-start | bytes 12296 | tf_op jit(solution)/shard_map/ppermute | solution.py:13
  (3 other events, 6.9 us)
